TPU v7x, 256 devices: a whole 4x4x8 slice. The times are simulated.
256 devices in a mesh: ka: 16 (over z, y_lo), band: 8 (over x, y_hi), ga: 2 (over core).
Axes of the slice: x: 4, y: 4 (y_hi: 2, y_lo: 2; y = y_hi * 2 + y_lo), z: 8, core: 2. Of those that a mesh axis runs over, the one named last changes fastest.
Arguments:
- pair_density: bfloat16 [8, 256, 8, 2048], P(None, ('ka', 'band')), may hold values from -4 to 4
- valence_energy: float32 [8, 8], replicated, may hold values from -6 to -1
- conduction_energy: float32 [8, 256], replicated, may hold values from 0.5 to 12
- star_map: int32 [64], replicated, may hold values from 0 to 7, as said below
- op_of_k: int32 [64], replicated, may hold values from 0 to 47
- perm_lists: int32 [48, 2048], replicated, may hold values from 0 to 2047, as said below
- cond_top: int32 [64], replicated, may hold values from 128 to 256
Outputs:
- chi: float32 [1, 2048, 2048], P(None, ('band', 'ga'), 'ka')
Inputs may be any that keep to these rules, and one draw needn't show every extreme that they name: `star_map`: every irreducible point is named by at least one full-zone k-point. `perm_lists`: each row is a permutation of 0 .. 2047 that maps every aligned block of 128 slots onto itself.
All inputs are finite; a program needn't handle non-finite values.
Results may differ from a plain program's by a relative error of at most 0.0015.
Values may be sent and summed in bfloat16 or wider, within the bound.
No kernel may reach another device: no remote copies, remote signals or barrier semaphores. Data moves between devices by JAX's collectives and lax.ppermute only.
A program may use at most 128 MiB of HBM per device.

v0:
```python
import jax
import jax.numpy as jnp
from jax import lax
from jax.sharding import PartitionSpec as P

NG = 2048
GB = 128
KI = 8
KF = 64
NF = 1
freq_step = 2.0


def rotate_batch(picked, perm_rows):
    k_count = picked.shape[0]
    blocks = NG // GB
    local = perm_rows.reshape(k_count, blocks, GB) - (jnp.arange(blocks) * GB)[None, :, None]
    onehot = (local[..., None] == jnp.arange(GB)[None, None, None, :]).astype(jnp.bfloat16)
    shaped = picked.reshape(k_count, -1, blocks, GB)
    moved = jnp.einsum("krbi,kboi->krbo", shaped, onehot, preferred_element_type=jnp.float32)
    return moved.astype(jnp.bfloat16).reshape(picked.shape)


def on_device(
    pair_density, valence_energy, conduction_energy, star_map, op_of_k, perm_lists, cond_top
):
    ka_count = lax.axis_size("ka")
    band_count = lax.axis_size("band")
    ga_count = lax.axis_size("ga")
    ka_index = lax.axis_index("ka")
    band_index = lax.axis_index("band")
    ga_index = lax.axis_index("ga")
    k_local = KF // ka_count
    cond_piece = pair_density.shape[1]
    my_points = ka_index * k_local + jnp.arange(k_local)
    stars = jnp.take(star_map, my_points)
    tops = jnp.take(cond_top, my_points)
    whole = lax.all_gather(pair_density, "ka", axis=1, tiled=True)
    picked = jnp.take(whole, stars, axis=0)
    my_perms = jnp.take(perm_lists, jnp.take(op_of_k, my_points), axis=0)
    rotated = rotate_batch(picked, my_perms)
    cond_table = conduction_energy.reshape(KI, ka_count, band_count, cond_piece)
    cond_table = lax.dynamic_slice_in_dim(cond_table, band_index, 1, 2).reshape(
        KI, ka_count * cond_piece
    )
    cond_local = jnp.take(cond_table, stars, axis=0)
    val_local = jnp.take(valence_energy, stars, axis=0)
    band_global = (
        jnp.arange(ka_count)[:, None] * band_count + band_index
    ) * cond_piece + jnp.arange(cond_piece)[None, :]
    band_global = band_global.reshape(ka_count * cond_piece)
    mask = (band_global[None, :] < tops[:, None]).astype(jnp.float32)[None, :, :, None]
    omega = freq_step * jnp.arange(NF).astype(jnp.float32)
    omega_sq = (omega * omega)[:, None, None, None]
    diff = val_local[:, None, :] - cond_local[:, :, None]
    weight = 4.0 / KF * diff[None] / (diff[None] * diff[None] + omega_sq) * mask
    product = weight[..., None] * rotated[None].astype(jnp.float32)
    scaled_hi = product.astype(jnp.bfloat16)
    hi_back = lax.optimization_barrier(scaled_hi).astype(jnp.float32)
    scaled_lo = (product - hi_back).astype(jnp.bfloat16)
    pair_rows = rotated.shape[0] * rotated.shape[1] * rotated.shape[2]
    flat_scaled = jnp.stack(
        [scaled_hi.reshape(NF, pair_rows, NG), scaled_lo.reshape(NF, pair_rows, NG)]
    )
    flat = rotated.reshape(pair_rows, NG)
    slab = NG // (band_count * ga_count)
    row_part = flat.reshape(pair_rows, band_count, ga_count, slab)
    row_part = lax.dynamic_slice_in_dim(row_part, ga_index, 1, 2).reshape(
        pair_rows, band_count * slab
    )
    partial_value = jnp.einsum(
        "rg,sfrh->fgh", row_part, flat_scaled, preferred_element_type=jnp.float32
    )
    column_sums = lax.psum_scatter(partial_value, "ka", scatter_dimension=2, tiled=True)
    return lax.psum_scatter(column_sums, "band", scatter_dimension=1, tiled=True)


def solution(mesh):
    return jax.shard_map(
        on_device,
        mesh=mesh,
        in_specs=(P(None, ("ka", "band"), None, None), P(), P(), P(), P(), P(), P()),
        out_specs=P(None, ("band", "ga"), "ka"),
        check_vma=False,
    )
```

profile of v0, /device:TPU:2, one launch (start us, length us, event | category | flops | bytes accessed | tf_op | source)
XLA Modules:
  0.0 547.9 jit_solution(13602813167420612139)
XLA Ops:
  6.5 0.0 copy-start
  6.5 0.0 all-gather.2.cloned.1.call-start
  6.5 0.7 all-gather.2.cloned.1.call-update
  7.3 0.0 reduce-scatter.3.cloned.1.call-start
  7.3 1.3 gather_fusion.6
  8.6 1.3 gather_fusion.5
  9.9 1.3 gather_fusion.4
  11.2 0.1 iota_add_fusion
  11.3 0.1 add.71
  11.4 0.8 copy.11
  12.3 0.1 copy.12
  12.3 1.2 gather_fusion
  13.6 0.6 gather_fusion.1
  14.2 0.1 compare_convert_fusion
  14.2 0.1 broadcast_select_fusion.1
  14.3 0.1 broadcast_select_fusion
  14.4 0.1 fusion.6
  14.5 0.1 mul.115
  14.6 0.0 copy-done
  14.6 0.6 gather_fusion.2
  15.2 0.1 fusion.7
  15.3 179.3 %all-gather.2.cloned.1.call-done = bf16[8,32,8,2048]{3,2,1,0:T(8,128)(2,1)} async-done(((bf16[8,2,8,2048]{3,2,1,0:T(8,128)(2,1)}), bf16[8,32,8,2048]{3,2,1,0:T(8,128)(2,1)}) %all-gather.2.cloned.1.call-update) | async-done | bytes 8388624 | tf_op jit(solution)/shard_map/all_gather | solution.py:38
  194.5 6.2 %gather_fusion.3 = bf16[4,32,8,2048]{3,2,1,0:T(8,128)(2,1)} fusion(bf16[8,32,8,2048]{3,2,1,0:T(8,128)(2,1)} %all-gather.2.cloned.1.call-done, s32[1024]{0:T(1024)S(1)} %pad_clamp_fusion.1), kind=kCustom, calls=%fused_computation.6 | custom fusion | bytes 8388624 | tf_op jit(solution)/shard_map/jit(_take)/gather | solution.py:39
  200.7 3.6 copy.20
  204.3 3.7 convert_bitcast_fusion
  208.0 6.4 %copy.16 = bf16[4,256,16,128]{3,1,0,2:T(8,128)(2,1)} copy(bf16[4,256,16,128]{1,3,2,0:T(8,128)(2,1)} %convert_bitcast_fusion) | data formatting | bytes 8388608 | tf_op jit(solution)/shard_map/convert_element_type | solution.py:21
  214.4 8.4 %copy.14 = f32[4,256,16,128]{3,2,1,0:T(8,128)} copy(bf16[4,256,16,128]{1,3,2,0:T(8,128)(2,1)} %convert_bitcast_fusion) | data formatting | bytes 12582912 | tf_op jit(solution)/shard_map/convert_element_type | solution.py:57
  222.7 9.3 %reshape.255 = f32[1,4,32,8,2048]{4,3,2,1,0:T(8,128)} reshape(f32[4,256,16,128]{3,2,1,0:T(8,128)} %copy.14) | data formatting | bytes 16777216 | tf_op jit(solution)/shard_map/convert_element_type | solution.py:57
  232.0 9.2 %reshape.254 = f32[1,1024,2048]{2,1,0:T(8,128)} reshape(f32[4,256,16,128]{3,2,1,0:T(8,128)} %copy.14) | data formatting | bytes 16777216 | tf_op jit(solution)/shard_map/convert_element_type | solution.py:57
  241.3 1.7 constant_dynamic-slice_fusion
  243.0 2.6 copy.17
  245.6 0.0 slice-start
  245.6 4.0 multiply_convert_fusion.1
  249.7 0.0 slice-start.1
  249.7 6.5 %subtract_convert_fusion = bf16[1,4,32,8,2048]{4,3,2,1,0:T(8,128)(2,1)} fusion(bf16[1,4,32,8,2048]{4,3,2,1,0:T(8,128)(2,1)S(1)} %multiply_convert_fusion.1, f32[1,4,32,8,2048]{4,3,2,1,0:T(8,128)} %reshape.255, f32[4,32,8]{2,1,0:T(8,128)S(1)} %fusion.6), kind=kLoop, calls=%fused_computation.8 | loop fusion | flops 8388608 | bytes 16781312 | tf_op jit(solution)/shard_map/convert_element_type | solution.py:60
  256.2 0.0 slice-done
  256.2 0.0 slice-done.1
  256.2 0.5 fusion
  256.7 7.4 %convert_reduce_fusion = bf16[1024,2048]{1,0:T(8,128)(2,1)} fusion(bf16[1,1,1024,2048]{3,2,1,0:T(8,128)(2,1)} %bitcast.31, bf16[1,1,1024,2048]{3,2,1,0:T(8,128)(2,1)S(1)} %fusion), kind=kLoop, calls=%fused_computation.7 | loop fusion | flops 18874368 | bytes 12582912 | tf_op jit(solution)/shard_map/rg,sfrh->fgh/reduce_sum | solution.py:71
  264.1 10.7 %convolution_bitcast_fusion = f32[1,1024,2048]{1,2,0:T(8,128)} fusion(bf16[1024,2048]{1,0:T(8,128)(2,1)} %convert_reduce_fusion, bf16[1024,1024]{0,1:T(8,128)(2,1)} %bitcast.35), kind=kOutput, calls=%fused_computation.11 | convolution fusion | flops 4294967296 | bytes 14680064 | tf_op jit(solution)/shard_map/rg,sfrh->fgh/dot_general | solution.py:71
  274.8 0.0 copy-start.1
  274.8 0.0 reduce-scatter.3.cloned.1.call-update
  274.8 0.0 reduce-scatter.5.cloned.1.call-start
  274.9 183.7 %reduce-scatter.3.cloned.1.call-done = f32[1,1024,128]{1,2,0:T(8,128)} async-done(((f32[1,1024,2048]{1,2,0:T(8,128)}), f32[1,1024,128]{1,2,0:T(8,128)}) %reduce-scatter.3.cloned.1.call-update) | async-done | bytes 524304 | tf_op jit(solution)/shard_map/reduce_scatter | solution.py:74
  458.6 0.0 reduce-scatter.5.cloned.1.call-update
  458.6 81.2 %reduce-scatter.5.cloned.1.call-done = f32[1,128,128]{1,2,0:T(8,128)} async-done(((f32[1,1024,128]{1,2,0:T(8,128)}), f32[1,128,128]{1,2,0:T(8,128)}) %reduce-scatter.5.cloned.1.call-update) | async-done | bytes 65552 | tf_op jit(solution)/shard_map/reduce_scatter | solution.py:75
  539.8 1.6 copy.18
  541.3 0.0 copy-done.1
  (10 shorter events, 0.1 us)
Async XLA Ops:
  6.5 8.1 %copy-start = (s32[48,2048]{1,0:T(8,128)S(1)}, s32[48,2048]{1,0:T(8,128)}, u32[]{:S(2)}) copy-start(s32[48,2048]{1,0:T(8,128)} %param.14) | copy-start | bytes 1179652
  6.5 188.0 %all-gather.2.cloned.1.call-start = ((), (), s32[]{:S(2)}) async-start(), calls=%async_computation.2 | async-start | bytes 8912896 | tf_op jit(solution)/shard_map/all_gather | solution.py:38
  7.3 451.3 %reduce-scatter.3.cloned.1.call-start = ((), (), s32[]{:S(2)}) async-start(), calls=%async_computation.3 | async-start | bytes 8912896 | tf_op jit(solution)/shard_map/reduce_scatter | solution.py:74
  245.6 10.5 %slice-start = ((s8[8388608]{0:T(1024)(128)(4,1)}), s8[4194304]{0:T(1024)(128)(4,1)S(1)}, s32[]{:S(2)}) async-start(s8[8388608]{0:T(1024)(128)(4,1)} %bitcast.29), calls=%async_computation.5 | async-start | bytes 8388608
  249.7 6.5 %slice-start.1 = ((s8[8388608]{0:T(1024)(128)(4,1)}), s8[4194304]{0:T(1024)(128)(4,1)S(1)}, s32[]{:S(2)}) async-start(s8[8388608]{0:T(1024)(128)(4,1)} %bitcast.29), calls=%async_computation.6 | async-start | bytes 8388608
  274.8 266.5 %copy-start.1 = (s32[48,2048]{1,0:T(8,128)S(1)}, s32[48,2048]{1,0:T(8,128)}, u32[]{:S(2)}) copy-start(s32[48,2048]{1,0:T(8,128)} %param.14) | copy-start | bytes 1179652
  274.8 264.9 %reduce-scatter.5.cloned.1.call-start = ((), (), s32[]{:S(2)}) async-start(), calls=%async_computation.4 | async-start | bytes 589824 | tf_op jit(solution)/shard_map/reduce_scatter | solution.py:75
Sparse Core Ops, SparseCore 0:
  9.1 185.3 all-gather.1
  274.9 183.5 reduce-scatter.2
  462.5 77.2 reduce-scatter.4
where the time goes:
time: 549 us; the launch traced here: 548 us
  waiting for transfers between devices  445 us (81%)
  local copies, waits for them, and re-layouts  56.3 us (10%)
  other arithmetic  18.9 us (3%)
  matrix products  14.4 us (3%)
  between operations  13.3 us (2%)
    reduce_scatter x1, waiting for transfers between devices, on_device(): lax.psum_scatter(partial_value, 'ka', scatter_dimension=2, tiled=True)  184 us
    all_gather x1, waiting for transfers between devices, on_device(): whole = lax.all_gather(pair_density, 'ka', axis=1, tiled=True)  179 us
    reduce_scatter x1, waiting for transfers between devices, on_device(): lax.psum_scatter(column_sums, 'band', scatter_dimension=1, tiled=True)  81.2 us
    convert_element_type x3, local copies, waits for them, and re-layouts, on_device(): product = weight[..., None] * rotated[None].astype(jnp.float32)  26.9 us
  transfers between devices with their start and end apart: 3, of which 3 were waited for; matrix products, arithmetic and copies ran while one was open for 1% of the time, Pallas kernels for 0%

commit v1 on v0

--- a/solution.py
+++ b/solution.py
@@ -35,7 +35,9 @@
     my_points = ka_index * k_local + jnp.arange(k_local)
     stars = jnp.take(star_map, my_points)
     tops = jnp.take(cond_top, my_points)
-    whole = lax.all_gather(pair_density, "ka", axis=1, tiled=True)
+    whole = jnp.concatenate(
+        lax.all_to_all(jnp.stack([pair_density] * lax.axis_size("ka")), "ka", 0, 0), axis=1
+    )
     picked = jnp.take(whole, stars, axis=0)
     my_perms = jnp.take(perm_lists, jnp.take(op_of_k, my_points), axis=0)
     rotated = rotate_batch(picked, my_perms)

time: 549 us -> 577 us (1.051)
  local copies, waits for them, and re-layouts: 56.3 us -> 66.6 us
  starting transfers between devices: 0.08 us -> 9.86 us
  waiting for transfers between devices: 445 us -> 452 us
    all_to_all x0 -> x1, waiting for transfers between devices: none -> 187 us  [on_device(): lax.all_to_all(jnp.stack([pair_density] * lax.axis_size('ka')), 'ka', 0, 0)]
    all_gather x1 -> x0, waiting for transfers between devices: 179 us -> none  [on_device(): whole = lax.all_gather(pair_density, 'ka', axis=1, tiled=True)]
    all_to_all x0 -> x1, starting transfers between devices: none -> 9.78 us  [on_device(): lax.all_to_all(jnp.stack([pair_density] * lax.axis_size('ka')), 'ka', 0, 0)]
    all_to_all x0 -> x1, local copies, waits for them, and re-layouts: none -> 8.28 us  [on_device(): lax.all_to_all(jnp.stack([pair_density] * lax.axis_size('ka')), 'ka', 0, 0)]
where the time goes in v1:
time: 577 us; the launch traced here: 576 us
  waiting for transfers between devices  452 us (78%)
  local copies, waits for them, and re-layouts  66.6 us (12%)
  other arithmetic  19.4 us (3%)
  matrix products  14.2 us (2%)
  between operations  13.6 us (2%)
  starting transfers between devices  9.86 us (2%)
    all_to_all x1, waiting for transfers between devices, on_device(): lax.all_to_all(jnp.stack([pair_density] * lax.axis_size('ka')), 'ka', 0, 0)  187 us
    reduce_scatter x1, waiting for transfers between devices, on_device(): lax.psum_scatter(partial_value, 'ka', scatter_dimension=2, tiled=True)  184 us
    reduce_scatter x1, waiting for transfers between devices, on_device(): lax.psum_scatter(column_sums, 'band', scatter_dimension=1, tiled=True)  81.2 us
    convert_element_type x3, local copies, waits for them, and re-layouts, on_device(): product = weight[..., None] * rotated[None].astype(jnp.float32)  26.9 us
  transfers between devices with their start and end apart: 3, of which 3 were waited for; matrix products, arithmetic and copies ran while one was open for 1% of the time, Pallas kernels for 0%

profile of v1, /device:TPU:2, one launch (start us, length us, event | category | flops | bytes accessed | tf_op | source)
XLA Modules:
  0.0 575.9 jit_solution(12356700002823252195)
XLA Ops:
  6.5 0.0 copy-start
  6.5 5.4 stack.8
  11.9 0.0 copy-start.2
  11.9 0.0 copy-start.3
  11.9 0.0 copy-start.4
  11.9 0.0 copy-start.6
  11.9 0.0 copy-start.5
  12.0 9.8 %all-to-all-start = ((bf16[16,8,2,8,2048]{4,3,2,1,0:T(8,128)(2,1)}), bf16[16,8,2,8,2048]{4,3,2,1,0:T(8,128)(2,1)}, u32[]{:S(2)}, u32[]{:S(2)}) async-start(bf16[16,8,2,8,2048]{4,3,2,1,0:T(8,128)(2,1)} %stack.8), calls=%async_computation | async-start | bytes 16777216 | tf_op jit(solution)/shard_map/all_to_all | solution.py:39
  21.7 0.0 reduce-scatter.3.cloned.1.call-start
  21.8 0.0 copy-done.2
  21.8 0.6 gather_fusion.6
  22.5 0.0 copy-done.3
  22.5 0.6 gather_fusion.5
  23.1 0.0 copy-done.4
  23.1 0.6 gather_fusion.4
  23.8 0.1 iota_add_fusion
  23.8 0.1 add.71
  23.9 0.0 copy-done.6
  23.9 0.1 copy.18
  24.1 0.1 copy.19
  24.2 0.0 copy-done.5
  24.2 0.6 gather_fusion
  24.8 0.6 gather_fusion.1
  25.3 0.1 compare_convert_fusion
  25.4 0.1 broadcast_select_fusion.1
  25.5 0.1 broadcast_select_fusion
  25.6 0.1 fusion.7
  25.7 0.1 mul.115
  25.8 0.0 copy-done
  25.8 0.6 gather_fusion.2
  26.4 0.1 fusion.8
  26.4 187.1 %all-to-all-done = bf16[16,8,2,8,2048]{4,3,2,1,0:T(8,128)(2,1)} async-done(((bf16[16,8,2,8,2048]{4,3,2,1,0:T(8,128)(2,1)}), bf16[16,8,2,8,2048]{4,3,2,1,0:T(8,128)(2,1)}, u32[]{:S(2)}, u32[]{:S(2)}) %all-to-all-start) | async-done | bytes 8388640 | tf_op jit(solution)/shard_map/all_to_all | solution.py:39
  213.5 8.3 %copy.20 = bf16[16,8,2,8,2048]{4,3,2,0,1:T(8,128)(2,1)} copy(bf16[16,8,2,8,2048]{4,3,2,1,0:T(8,128)(2,1)} %all-to-all-done) | data formatting | bytes 16777216 | tf_op jit(solution)/shard_map/all_to_all | solution.py:39
  221.8 6.2 %gather_fusion.3 = bf16[4,32,8,2048]{3,2,1,0:T(8,128)(2,1)} fusion(bf16[8,32,8,2048]{3,2,1,0:T(8,128)(2,1)} %bitcast.36, s32[1024]{0:T(1024)S(1)} %pad_clamp_fusion.1), kind=kCustom, calls=%fused_computation.6 | custom fusion | bytes 8388624 | tf_op jit(solution)/shard_map/jit(_take)/gather | solution.py:41
  227.9 3.6 copy.28
  231.5 0.5 bitcast_select_fusion
  232.0 3.5 convert_bitcast_fusion
  235.5 6.4 %copy.24 = bf16[4,256,16,128]{3,1,0,2:T(8,128)(2,1)} copy(bf16[4,256,16,128]{1,3,2,0:T(8,128)(2,1)} %convert_bitcast_fusion) | data formatting | bytes 8388608 | tf_op jit(solution)/shard_map/convert_element_type | solution.py:21
  241.9 8.4 %copy.22 = f32[4,256,16,128]{3,2,1,0:T(8,128)} copy(bf16[4,256,16,128]{1,3,2,0:T(8,128)(2,1)} %convert_bitcast_fusion) | data formatting | bytes 12582912 | tf_op jit(solution)/shard_map/convert_element_type | solution.py:59
  250.3 9.3 %reshape.265 = f32[1,4,32,8,2048]{4,3,2,1,0:T(8,128)} reshape(f32[4,256,16,128]{3,2,1,0:T(8,128)} %copy.22) | data formatting | bytes 16777216 | tf_op jit(solution)/shard_map/convert_element_type | solution.py:59
  259.5 9.2 %reshape.264 = f32[1,1024,2048]{2,1,0:T(8,128)} reshape(f32[4,256,16,128]{3,2,1,0:T(8,128)} %copy.22) | data formatting | bytes 16777216 | tf_op jit(solution)/shard_map/convert_element_type | solution.py:59
  268.8 1.7 constant_dynamic-slice_fusion
  270.5 2.6 copy.25
  273.1 0.0 slice-start
  273.1 4.0 multiply_convert_fusion.1
  277.2 0.0 slice-start.1
  277.2 6.5 %subtract_convert_fusion = bf16[1,4,32,8,2048]{4,3,2,1,0:T(8,128)(2,1)} fusion(bf16[1,4,32,8,2048]{4,3,2,1,0:T(8,128)(2,1)S(1)} %multiply_convert_fusion.1, f32[1,4,32,8,2048]{4,3,2,1,0:T(8,128)} %reshape.265, f32[4,32,8]{2,1,0:T(8,128)S(1)} %fusion.7), kind=kLoop, calls=%fused_computation.8 | loop fusion | flops 8388608 | bytes 16781312 | tf_op jit(solution)/shard_map/convert_element_type | solution.py:62
  283.7 0.0 slice-done
  283.7 0.0 slice-done.1
  283.7 0.5 fusion
  284.2 7.4 %convert_reduce_fusion = bf16[1024,2048]{1,0:T(8,128)(2,1)} fusion(bf16[1,1,1024,2048]{3,2,1,0:T(8,128)(2,1)} %bitcast.37, bf16[1,1,1024,2048]{3,2,1,0:T(8,128)(2,1)S(1)} %fusion), kind=kLoop, calls=%fused_computation.7 | loop fusion | flops 18874368 | bytes 12582912 | tf_op jit(solution)/shard_map/rg,sfrh->fgh/reduce_sum | solution.py:73
  291.6 10.7 %convolution_bitcast_fusion = f32[1,1024,2048]{1,2,0:T(8,128)} fusion(bf16[1024,2048]{1,0:T(8,128)(2,1)} %convert_reduce_fusion, bf16[1024,1024]{0,1:T(8,128)(2,1)} %bitcast.41), kind=kOutput, calls=%fused_computation.11 | convolution fusion | flops 4294967296 | bytes 14680064 | tf_op jit(solution)/shard_map/rg,sfrh->fgh/dot_general | solution.py:73
  302.3 0.0 copy-start.1
  302.3 0.0 reduce-scatter.3.cloned.1.call-update
  302.3 0.0 reduce-scatter.5.cloned.1.call-start
  302.3 184.0 %reduce-scatter.3.cloned.1.call-done = f32[1,1024,128]{1,2,0:T(8,128)} async-done(((f32[1,1024,2048]{1,2,0:T(8,128)}), f32[1,1024,128]{1,2,0:T(8,128)}) %reduce-scatter.3.cloned.1.call-update) | async-done | bytes 524304 | tf_op jit(solution)/shard_map/reduce_scatter | solution.py:76
  486.4 0.0 reduce-scatter.5.cloned.1.call-update
  486.4 81.2 %reduce-scatter.5.cloned.1.call-done = f32[1,128,128]{1,2,0:T(8,128)} async-done(((f32[1,1024,128]{1,2,0:T(8,128)}), f32[1,128,128]{1,2,0:T(8,128)}) %reduce-scatter.5.cloned.1.call-update) | async-done | bytes 65552 | tf_op jit(solution)/shard_map/reduce_scatter | solution.py:77
  567.5 1.6 copy.26
  569.1 0.0 copy-done.1
  (10 shorter events, 0.1 us)
Async XLA Ops:
  6.5 19.2 %copy-start = (s32[48,2048]{1,0:T(8,128)S(1)}, s32[48,2048]{1,0:T(8,128)}, u32[]{:S(2)}) copy-start(s32[48,2048]{1,0:T(8,128)} %param.14) | copy-start | bytes 1179652
  11.9 9.9 %copy-start.2 = (s32[64]{0:T(128)S(1)}, s32[64]{0:T(128)}, u32[]{:S(2)}) copy-start(s32[64]{0:T(128)} %param.13) | copy-start | bytes 772
  11.9 10.5 %copy-start.3 = (s32[64]{0:T(128)S(1)}, s32[64]{0:T(128)}, u32[]{:S(2)}) copy-start(s32[64]{0:T(128)} %param.15) | copy-start | bytes 772
  11.9 11.2 %copy-start.4 = (s32[64]{0:T(128)S(1)}, s32[64]{0:T(128)}, u32[]{:S(2)}) copy-start(s32[64]{0:T(128)} %param.12) | copy-start | bytes 772
  11.9 12.0 %copy-start.6 = (f32[8,256]{1,0:T(8,128)S(1)}, f32[8,256]{1,0:T(8,128)}, u32[]{:S(2)}) copy-start(f32[8,256]{1,0:T(8,128)} %param.11) | copy-start | bytes 24580
  11.9 12.3 %copy-start.5 = (f32[8,8]{1,0:T(8,128)S(1)}, f32[8,8]{1,0:T(8,128)}, u32[]{:S(2)}) copy-start(f32[8,8]{1,0:T(8,128)} %param.10) | copy-start | bytes 772
  12.0 201.5 %all-to-all-start = ((bf16[16,8,2,8,2048]{4,3,2,1,0:T(8,128)(2,1)}), bf16[16,8,2,8,2048]{4,3,2,1,0:T(8,128)(2,1)}, u32[]{:S(2)}, u32[]{:S(2)}) async-start(bf16[16,8,2,8,2048]{4,3,2,1,0:T(8,128)(2,1)} %stack.8), calls=%async_computation | async-start | bytes 16777216 | tf_op jit(solution)/shard_map/all_to_all | solution.py:39
  21.7 464.6 %reduce-scatter.3.cloned.1.call-start = ((), (), s32[]{:S(2)}) async-start(), calls=%async_computation.3 | async-start | bytes 8912896 | tf_op jit(solution)/shard_map/reduce_scatter | solution.py:76
  273.1 10.5 %slice-start = ((s8[8388608]{0:T(1024)(128)(4,1)}), s8[4194304]{0:T(1024)(128)(4,1)S(1)}, s32[]{:S(2)}) async-start(s8[8388608]{0:T(1024)(128)(4,1)} %bitcast.34), calls=%async_computation.5 | async-start | bytes 8388608
  277.2 6.5 %slice-start.1 = ((s8[8388608]{0:T(1024)(128)(4,1)}), s8[4194304]{0:T(1024)(128)(4,1)S(1)}, s32[]{:S(2)}) async-start(s8[8388608]{0:T(1024)(128)(4,1)} %bitcast.34), calls=%async_computation.6 | async-start | bytes 8388608
  302.3 266.8 %copy-start.1 = (s32[48,2048]{1,0:T(8,128)S(1)}, s32[48,2048]{1,0:T(8,128)}, u32[]{:S(2)}) copy-start(s32[48,2048]{1,0:T(8,128)} %param.14) | copy-start | bytes 1179652
  302.3 265.2 %reduce-scatter.5.cloned.1.call-start = ((), (), s32[]{:S(2)}) async-start(), calls=%async_computation.4 | async-start | bytes 589824 | tf_op jit(solution)/shard_map/reduce_scatter | solution.py:77
Sparse Core Ops, SparseCore 0:
  302.4 183.8 reduce-scatter.2
  490.2 77.2 reduce-scatter.4
